TPU v7x, 32 devices: a whole 2x2x4 slice. The times are simulated.
32 devices in a mesh: tok: 8 (over z, x), grp: 4 (over y, core).
Axes of the slice: x: 2, y: 2, z: 4, core: 2. Of those that a mesh axis runs over, the one named last changes fastest.
Arguments:
- queries: bfloat16 [1536, 2048], P('tok', 'grp'), may hold values from -72 to 72
- new_keys: bfloat16 [1536, 2048], P('tok', 'grp'), may hold values from -8 to 8
- new_values: bfloat16 [1536, 2048], P('tok', 'grp'), may hold values from -6 to 6
- residual: bfloat16 [1536, 2048], P('tok', 'grp'), may hold values from -6 to 6
- w_out: bfloat16 [2048, 2048], P('grp'), may hold values from -0.125 to 0.125
- leaf_keys: bfloat16 [8, 512, 2048], P('tok', None, 'grp'), may hold values from -6 to 6
- leaf_values: bfloat16 [8, 512, 2048], P('tok', None, 'grp'), may hold values from -6 to 6
- upper_keys: bfloat16 [6, 1024, 2048], P(None, 'tok', 'grp'), may hold values from -8 to 8
- upper_values: bfloat16 [6, 1024, 2048], P(None, 'tok', 'grp'), may hold values from -6 to 6
- req_len: int32 [8], replicated, may hold values from 48 to 192, as said below
- leaf_mid: int32 [8], replicated, may hold values from 0 to 3
- mid_root: int32 [4], replicated, may hold values from 0 to 1, as said below
- upper_len: int32 [6], replicated, may hold values from 256 to 1024, as said below
- leaf_len: int32 [8], replicated, may hold values from 128 to 512, as said below
Outputs:
- hidden_out: bfloat16 [1536, 2048], P('tok', 'grp')
Inputs may be any that keep to these rules, and one draw needn't show every extreme that they name: `req_len`: some request has exactly 192 new tokens. `mid_root`: each root is the parent of 2 mids. `upper_len`: the first 2 entries are roots and equal 1024. `leaf_len`: some leaf has exactly 512 positions.
All inputs are finite; a program needn't handle non-finite values.
Results may differ from a plain program's by a relative error of at most 0.008.
Values may be sent and summed in bfloat16 or wider, within the bound.
No kernel may reach another device: no remote copies, remote signals or barrier semaphores. Data moves between devices by JAX's collectives and lax.ppermute only.
A program may use at most 64 MiB of HBM per device.

v0:
```python
import jax
import jax.numpy as jnp
from jax import lax
from jax.sharding import PartitionSpec as P

HEAD_DIM = 128
NEG_FILL = -1e30


def partial_attention(query_rows, key_rows, values, allowed, head_count):
    head_width = query_rows.shape[1] // head_count
    parts = []
    for head in range(head_count):
        cols = slice(head * head_width, (head + 1) * head_width)
        scores = lax.dot_general(
            query_rows[:, cols],
            key_rows[:, cols],
            (((1,), (1,)), ((), ())),
            preferred_element_type=jnp.float32,
        ) * head_width ** (-0.5)
        scores = jnp.where(allowed, scores, NEG_FILL)
        row_max = jnp.max(scores, axis=1, keepdims=True)
        exp_scores = jnp.where(allowed, jnp.exp(scores - row_max), 0.0)
        row_total = jnp.sum(exp_scores, axis=1, keepdims=True)
        weighted = jnp.dot(
            exp_scores.astype(jnp.bfloat16), values[:, cols], preferred_element_type=jnp.float32
        )
        parts.append((row_max, row_total, weighted))
    return parts


def combine(earlier, latter):
    merged = []
    for (max_a, total_a, sum_a), (max_b, total_b, sum_b) in zip(earlier, latter):
        new_max = jnp.maximum(max_a, max_b)
        scale_a = jnp.exp(max_a - new_max)
        scale_b = jnp.exp(max_b - new_max)
        merged.append(
            (new_max, total_a * scale_a + total_b * scale_b, sum_a * scale_a + sum_b * scale_b)
        )
    return merged


def shards(
    queries,
    new_keys,
    new_values,
    residual,
    w_out,
    leaf_keys,
    leaf_values,
    upper_keys,
    upper_values,
    req_len,
    leaf_mid,
    mid_root,
    upper_len,
    leaf_len,
):
    dev_count = lax.axis_size("tok")
    my_index = lax.axis_index("tok")
    row_count = queries.shape[0]
    col_count = queries.shape[1]
    head_count = col_count // HEAD_DIM
    head_width = col_count // head_count
    mid_count = mid_root.shape[0]
    node_count = upper_len.shape[0]
    root_count = node_count - mid_count
    chunk = upper_keys.shape[1]
    owned = (jnp.arange(dev_count, dtype=jnp.int32) == my_index).astype(jnp.int32)
    my_length = jnp.sum(owned * req_len)
    my_mid = jnp.sum(owned * leaf_mid)
    my_leaf_len = jnp.sum(owned * leaf_len)
    my_root = jnp.sum((jnp.arange(mid_count) == my_mid).astype(jnp.int32) * mid_root)
    node_ids = jnp.arange(node_count)
    root_len = jnp.sum((node_ids == my_root).astype(jnp.int32) * upper_len)
    mid_len = jnp.sum((node_ids == root_count + my_mid).astype(jnp.int32) * upper_len)
    position = jnp.arange(row_count, dtype=jnp.int32)
    is_live = position < my_length
    leaf_count = leaf_keys.shape[1]
    local_keys = jnp.concatenate([leaf_keys[0], new_keys], axis=0)
    local_values = jnp.concatenate([leaf_values[0], new_values], axis=0)
    leaf_allowed = jnp.broadcast_to(
        (jnp.arange(leaf_count) < my_leaf_len)[None, :], (row_count, leaf_count)
    )
    new_allowed = (position[None, :] <= position[:, None]) & is_live[None, :]
    local_allowed = jnp.concatenate([leaf_allowed, new_allowed], axis=1)
    if dev_count * row_count * col_count * 4 <= 8 << 20:
        merged = query_plan(
            queries,
            local_keys,
            local_values,
            local_allowed,
            upper_keys,
            upper_values,
            leaf_mid,
            mid_root,
            upper_len,
            head_count,
            my_index,
            root_count,
            chunk,
        )
    else:
        merged = node_plan(
            queries,
            local_keys,
            local_values,
            local_allowed,
            upper_keys,
            upper_values,
            leaf_mid,
            mid_root,
            root_len,
            mid_len,
            head_count,
            root_count,
            chunk,
        )
    attended = jnp.concatenate([part[2] / part[1] for part in merged], axis=1)
    attention = jnp.where(is_live[:, None], attended, 0.0).astype(jnp.bfloat16)
    projected = jnp.dot(attention, w_out, preferred_element_type=jnp.float32)
    mixed = lax.psum_scatter(
        projected.astype(jnp.bfloat16), "grp", scatter_dimension=1, tiled=True
    ).astype(jnp.float32)
    return (residual.astype(jnp.float32) + mixed).astype(jnp.bfloat16)


def node_plan(
    queries,
    local_keys,
    local_values,
    local_allowed,
    upper_keys,
    upper_values,
    leaf_mid,
    mid_root,
    root_len,
    mid_len,
    head_count,
    root_count,
    chunk,
):
    dev_count = lax.axis_size("tok")
    col_count = queries.shape[1]
    dest_mid = leaf_mid.astype(jnp.int32)
    dest_root = jnp.take(mid_root, dest_mid).astype(jnp.int32)
    dest_nodes = jnp.stack([dest_root, root_count + dest_mid], axis=1)
    send = jnp.concatenate(
        [
            upper_keys.at[dest_nodes].get(mode="promise_in_bounds"),
            upper_values.at[dest_nodes].get(mode="promise_in_bounds"),
        ],
        axis=1,
    )
    received = lax.all_to_all(send, "tok", 0, 0, tiled=True)
    recv_keys = received[:, :2]
    recv_values = received[:, 2:]
    local_part = partial_attention(queries, local_keys, local_values, local_allowed, head_count)
    upper_pos = (
        jnp.arange(dev_count, dtype=jnp.int32)[:, None, None] * chunk
        + jnp.arange(chunk, dtype=jnp.int32)[None, None, :]
    )
    upper_limit = jnp.stack([root_len, mid_len])[None, :, None]
    upper_ok = (upper_pos < upper_limit).reshape(-1)
    upper_part = partial_attention(
        queries,
        recv_keys.reshape(-1, col_count),
        recv_values.reshape(-1, col_count),
        upper_ok[None, :],
        head_count,
    )
    return combine(local_part, upper_part)


def query_plan(
    queries,
    local_keys,
    local_values,
    local_allowed,
    upper_keys,
    upper_values,
    leaf_mid,
    mid_root,
    upper_len,
    head_count,
    my_index,
    root_count,
    chunk,
):
    dev_count = lax.axis_size("tok")
    row_count = queries.shape[0]
    col_count = queries.shape[1]
    head_width = col_count // head_count
    node_count = upper_keys.shape[0]
    scale = head_width ** (-0.5)
    all_queries = lax.all_gather(queries, "tok", axis=0, tiled=True)
    req_mid = leaf_mid.astype(jnp.int32)
    req_root = jnp.take(mid_root, req_mid).astype(jnp.int32)
    node_ids = jnp.arange(node_count, dtype=jnp.int32)
    node_used = (node_ids[None, :] == req_root[:, None]) | (
        node_ids[None, :] == root_count + req_mid[:, None]
    )
    pos_ok = (my_index * chunk + jnp.arange(chunk, dtype=jnp.int32))[None, :] < upper_len[:, None]
    seen = (node_used[:, :, None] & pos_ok[None, :, :]).reshape(dev_count, 1, node_count * chunk)
    flat_keys = upper_keys.reshape(node_count * chunk, col_count)
    flat_values = upper_values.reshape(node_count * chunk, col_count)
    upper_scores = []
    local_scores = []
    maxima = []
    for head in range(head_count):
        cols = slice(head * head_width, (head + 1) * head_width)
        scores = (
            lax.dot_general(
                all_queries[:, cols],
                flat_keys[:, cols],
                (((1,), (1,)), ((), ())),
                preferred_element_type=jnp.float32,
            )
            * scale
        )
        scores = jnp.where(seen, scores.reshape(dev_count, row_count, -1), NEG_FILL)
        upper_max = jnp.max(scores, axis=2)
        own = lax.dynamic_slice_in_dim(upper_max, my_index, 1, axis=0)
        mine = (
            lax.dot_general(
                queries[:, cols],
                local_keys[:, cols],
                (((1,), (1,)), ((), ())),
                preferred_element_type=jnp.float32,
            )
            * scale
        )
        mine = jnp.where(local_allowed, mine, NEG_FILL)
        own = jnp.maximum(own, jnp.max(mine, axis=1)[None, :])
        maxima.append(lax.dynamic_update_slice_in_dim(upper_max, own, my_index, axis=0))
        upper_scores.append(scores)
        local_scores.append(mine)
    row_max = lax.pmax(jnp.stack(maxima, axis=2), "tok")
    sums = []
    totals = []
    for head in range(head_count):
        cols = slice(head * head_width, (head + 1) * head_width)
        head_max = row_max[:, :, head : head + 1]
        exps = jnp.where(seen, jnp.exp(upper_scores[head] - head_max), 0.0)
        totals.append(jnp.sum(exps, axis=2))
        sums.append(
            jnp.dot(
                exps.reshape(dev_count * row_count, -1).astype(jnp.bfloat16),
                flat_values[:, cols],
                preferred_element_type=jnp.float32,
            )
        )
    upper_sum, upper_total = lax.psum_scatter(
        (
            jnp.concatenate(sums, axis=1),
            jnp.stack(totals, axis=2).reshape(dev_count * row_count, head_count),
        ),
        "tok",
        scatter_dimension=0,
        tiled=True,
    )
    own_max = lax.dynamic_index_in_dim(row_max, my_index, axis=0, keepdims=False)
    merged = []
    for head in range(head_count):
        cols = slice(head * head_width, (head + 1) * head_width)
        exps = jnp.where(
            local_allowed, jnp.exp(local_scores[head] - own_max[:, head : head + 1]), 0.0
        )
        total = jnp.sum(exps, axis=1, keepdims=True) + upper_total[:, head : head + 1]
        weighted = (
            jnp.dot(
                exps.astype(jnp.bfloat16), local_values[:, cols], preferred_element_type=jnp.float32
            )
            + upper_sum[:, cols]
        )
        merged.append((None, total, weighted))
    return merged


def solution(mesh):
    in_specs = (
        P("tok", "grp"),
        P("tok", "grp"),
        P("tok", "grp"),
        P("tok", "grp"),
        P("grp", None),
        P("tok", None, "grp"),
        P("tok", None, "grp"),
        P(None, "tok", "grp"),
        P(None, "tok", "grp"),
        P(),
        P(),
        P(),
        P(),
        P(),
    )
    out_specs = P("tok", "grp")
    return jax.shard_map(shards, mesh=mesh, in_specs=in_specs, out_specs=out_specs, check_vma=False)
```

profile of v0, /device:TPU:0, one launch (start us, length us, event | category | flops | bytes accessed | tf_op | source)
XLA Modules:
  0.0 299.4 jit_solution(17973138903810217957)
XLA Ops:
  15.2 2.0 fusion.134
  17.1 2.0 fusion.133
  19.2 2.0 fusion.132
  21.1 2.0 fusion.131
  23.1 33.2 %all-gather.2.cloned.1.call-done = bf16[1536,512]{1,0:T(8,128)(2,1)} async-done(((bf16[192,512]{1,0:T(8,128)(2,1)}), bf16[1536,512]{1,0:T(8,128)(2,1)}) %all-gather.2.cloned.1.call-update) | async-done | bytes 1572880 | tf_op jit(solution)/shard_map/all_gather | solution.py:197
  56.3 2.0 fusion.40
  61.9 4.7 %fusion = (f32[1536]{0:T(1024)S(1)}, f32[1536]{0:T(1024)S(1)}, f32[1536]{0:T(1024)S(1)}, f32[1536]{0:T(1024)S(1)}, f32[1536,768]{0,1:T(8,128)}) fusion(pred[1536,768]{0,1:T(32,128)(4,1)S(1)} %copy.27, f32[1536,768]{0,1:T(8,128)S(1)} %fusion.40, f32[1536,768]{0,1:T(8,128)S(1)} %fusion.42, f32[1536,768]{0,1:T(8,128)S(1)} %fusion.44, ...), kind=kOutput, calls=%fused_computation.9 | convolution fusion | flops 316139520 | bytes 20668416 | tf_op jit(solution)/shard_map/dot_general | solution.py:214
  67.4 35.0 %pmax.7 = f32[8,192,4]{1,0,2:T(8,128)S(1)} all-reduce(f32[8,192,4]{1,0,2:T(8,128)S(1)} %pad_maximum_fusion.5), channel_id=1, replica_groups=mesh['tok'=8,'grp'=4] {'tok'}, use_global_device_ids=true, to_apply=%region_10.11 | all-reduce | flops 6144 | bytes 49152 | tf_op jit(solution)/shard_map/pmax | solution.py:239
  102.7 4.9 %fusion.16 = f32[1536,128]{0,1:T(8,128)S(1)} fusion(pred[1536,768]{0,1:T(32,128)(4,1)} %copy-done.4, f32[1536,768]{0,1:T(8,128)} %copy-done.3, f32[1536]{0:T(1024)S(1)} %sub.94, bf16[768,512]{1,0:T(8,128)(2,1)} %bitcast.111), kind=kOutput, calls=%fused_computation.25 | convolution fusion | flops 307888128 | bytes 6887424 | tf_op jit(solution)/shard_map/dot_general | solution.py:248
  107.7 2.3 fusion.14
  110.0 5.4 %fusion.18 = f32[1536,128]{0,1:T(8,128)} fusion(pred[1536,768]{0,1:T(32,128)(4,1)S(1)} %copy-done.5, f32[1536,768]{0,1:T(8,128)} %get-tuple-element.31, f32[1536]{0:T(1024)S(1)} %sub.91, bf16[768,512]{1,0:T(8,128)(2,1)S(1)} %bitcast.113), kind=kOutput, calls=%fused_computation.26 | convolution fusion | flops 307888128 | bytes 6889472 | tf_op jit(solution)/shard_map/dot_general | solution.py:248
  115.5 4.7 %fusion.4 = (f32[1536]{0:T(1024)S(1)}, f32[1536]{0:T(1024)S(1)}, f32[1536]{0:T(1024)S(1)}, f32[1536]{0:T(1024)S(1)}) fusion(pred[1536,768]{0,1:T(32,128)(4,1)S(1)} %copy-done.5, f32[1536,768]{0,1:T(8,128)S(1)} %bitcast.80, f32[1536]{0:T(1024)S(1)} %sub.91, f32[1536]{0:T(1024)S(1)} %sub.100, f32[1536,768]{0,1:T(8,128)S(1)} %bitcast.74, f32[1536]{0:T(1024)S(1)} %sub.97, ...), kind=kLoop, calls=%fused_computation.14 | loop fusion | flops 23586816 | bytes 20103168 | tf_op jit(solution)/shard_map/reduce_sum | solution.py:246
  120.2 2.3 fusion.12
  123.9 3.5 %pad_maximum_fusion = f32[1536,512]{0,1:T(8,128)} fusion(f32[1536,128]{0,1:T(8,128)} %fusion.12, f32[1536,128]{0,1:T(8,128)} %fusion.14, f32[1536,128]{0,1:T(8,128)S(1)} %fusion.16, f32[1536,128]{0,1:T(8,128)} %fusion.18), kind=kLoop, calls=%fused_computation.13 | loop fusion | flops 2359296 | bytes 6291456 | tf_op jit(solution)/shard_map/concatenate | solution.py:256
  127.4 3.7 %copy.43 = f32[1536,512]{1,0:T(8,128)} copy(f32[1536,512]{0,1:T(8,128)} %pad_maximum_fusion) | data formatting | bytes 6291456
  131.3 2.0 fusion.32
  133.3 50.3 %reduce-scatter.12.cloned.1.call-done = f32[192,4]{1,0:T(8,128)} async-done(((f32[1536,4]{1,0:T(8,128)}), f32[192,4]{1,0:T(8,128)}) %reduce-scatter.12.cloned.1.call-update) | async-done | bytes 3088
  183.6 1.8 fusion.128
  187.6 73.3 %reduce-scatter.10.cloned.1.call-done = f32[192,512]{1,0:T(8,128)} async-done(((f32[1536,512]{1,0:T(8,128)}), f32[192,512]{1,0:T(8,128)}) %reduce-scatter.10.cloned.1.call-update) | async-done | bytes 393232 | tf_op jit(solution)/shard_map/reduce_scatter | solution.py:254
  260.9 1.5 fusion.28
  262.4 1.5 fusion.29
  266.5 2.1 convolution_convert_fusion
  268.6 22.5 %reduce-scatter.8.cloned.1.call-done = bf16[192,512]{1,0:T(8,128)(2,1)} async-done(((bf16[192,2048]{1,0:T(8,128)(2,1)}), bf16[192,512]{1,0:T(8,128)(2,1)}) %reduce-scatter.8.cloned.1.call-update) | async-done | bytes 196624 | tf_op jit(solution)/shard_map/reduce_scatter | solution.py:123
  291.2 1.7 add_convert_fusion
  (129 shorter events, 19.3 us)
Async XLA Ops:
  6.5 260.0 %copy-start = (bf16[512,2048]{1,0:T(8,128)(2,1)S(1)}, bf16[512,2048]{1,0:T(8,128)(2,1)}, u32[]{:S(2)}) copy-start(bf16[512,2048]{1,0:T(8,128)(2,1)} %param.18) | copy-start | bytes 6291460
  6.5 10.6 %copy-start.7 = (bf16[192,512]{1,0:T(8,128)(2,1)S(1)}, bf16[192,512]{1,0:T(8,128)(2,1)}, u32[]{:S(2)}) copy-start(bf16[192,512]{1,0:T(8,128)(2,1)} %param.15) | copy-start | bytes 589828
  6.5 49.8 %all-gather.2.cloned.1.call-start = ((), (), s32[]{:S(2)}) async-start(), calls=%async_computation.3 | async-start | bytes 1769472 | tf_op jit(solution)/shard_map/all_gather | solution.py:197
  7.3 176.3 %reduce-scatter.12.cloned.1.call-start = ((), (), s32[]{:S(2)}) async-start(), calls=%async_computation.6 | async-start | bytes 884736
  12.4 47.5 %copy-start.4 = (pred[1536,768]{0,1:T(32,128)(4,1)}, pred[1536,768]{0,1:T(32,128)(4,1)S(1)}, u32[]{:S(2)}) copy-start(pred[1536,768]{0,1:T(32,128)(4,1)S(1)} %copy.27) | copy-start | bytes 3538948
  15.1 4.0 %copy-start.17 = (pred[192]{0:T(512)(128)(4,1)}, pred[192]{0:T(512)(128)(4,1)S(1)}, u32[]{:S(2)}) copy-start(pred[192]{0:T(512)(128)(4,1)S(1)} %iota_compare_fusion.4) | copy-start | bytes 580
  61.9 4.7 %copy-start.3 = (f32[1536,768]{0,1:T(8,128)}, f32[1536,768]{0,1:T(8,128)S(1)}, u32[]{:S(2)}) copy-start(f32[1536,768]{0,1:T(8,128)S(1)} %fusion.44) | copy-start | bytes 14155780
  102.4 5.2 %slice-start.2 = ((s8[4718592]{0:T(1024)(128)(4,1)}), s8[524288]{0:T(1024)(128)(4,1)S(1)}, s32[]{:S(2)}) async-start(s8[4718592]{0:T(1024)(128)(4,1)} %bitcast.75), calls=%async_computation.9 | async-start | bytes 1048576
  102.7 5.0 %slice-start.3 = ((s8[4718592]{0:T(1024)(128)(4,1)}), s8[4194304]{0:T(1024)(128)(4,1)S(1)}, s32[]{:S(2)}) async-start(s8[4718592]{0:T(1024)(128)(4,1)} %bitcast.75), calls=%async_computation.10 | async-start | bytes 8388608
  102.7 5.0 %copy-start.5 = (pred[1536,768]{0,1:T(32,128)(4,1)S(1)}, pred[1536,768]{0,1:T(32,128)(4,1)}, u32[]{:S(2)}) copy-start(pred[1536,768]{0,1:T(32,128)(4,1)} %copy-done.4) | copy-start | bytes 3538948
  102.7 5.0 %copy-start.18 = (bf16[6,128,512]{2,1,0:T(8,128)(2,1)S(1)}, bf16[6,128,512]{2,1,0:T(8,128)(2,1)}, u32[]{:S(2)}) copy-start(bf16[6,128,512]{2,1,0:T(8,128)(2,1)} %param.22) | copy-start | bytes 2359300
  107.7 7.8 %slice-start = ((s8[4718592]{0:T(1024)(128)(4,1)}), s8[4194304]{0:T(1024)(128)(4,1)S(1)}, s32[]{:S(2)}) async-start(s8[4718592]{0:T(1024)(128)(4,1)} %bitcast.73), calls=%async_computation.7 | async-start | bytes 8388608
  107.7 7.8 %slice-start.4 = ((s8[4718592]{0:T(1024)(128)(4,1)}), s8[4194304]{0:T(1024)(128)(4,1)S(1)}, s32[]{:S(2)}) async-start(s8[4718592]{0:T(1024)(128)(4,1)} %bitcast.77), calls=%async_computation.11 | async-start | bytes 8388608
  107.7 7.8 %slice-start.6 = ((s8[4718592]{0:T(1024)(128)(4,1)}), s8[4194304]{0:T(1024)(128)(4,1)S(1)}, s32[]{:S(2)}) async-start(s8[4718592]{0:T(1024)(128)(4,1)} %bitcast.79), calls=%async_computation.13 | async-start | bytes 8388608
  110.0 5.4 %slice-start.1 = ((s8[4718592]{0:T(1024)(128)(4,1)}), s8[524288]{0:T(1024)(128)(4,1)S(1)}, s32[]{:S(2)}) async-start(s8[4718592]{0:T(1024)(128)(4,1)} %bitcast.73), calls=%async_computation.8 | async-start | bytes 1048576
  110.0 5.5 %slice-start.5 = ((s8[4718592]{0:T(1024)(128)(4,1)}), s8[524288]{0:T(1024)(128)(4,1)S(1)}, s32[]{:S(2)}) async-start(s8[4718592]{0:T(1024)(128)(4,1)} %bitcast.77), calls=%async_computation.12 | async-start | bytes 1048576
  110.0 5.5 %slice-start.7 = ((s8[4718592]{0:T(1024)(128)(4,1)}), s8[524288]{0:T(1024)(128)(4,1)S(1)}, s32[]{:S(2)}) async-start(s8[4718592]{0:T(1024)(128)(4,1)} %bitcast.79), calls=%async_computation.14 | async-start | bytes 1048576
  123.8 137.0 %reduce-scatter.10.cloned.1.call-start = ((), (), s32[]{:S(2)}) async-start(), calls=%async_computation.5 | async-start | bytes 3538944 | tf_op jit(solution)/shard_map/reduce_scatter | solution.py:254
  127.4 3.9 %copy-start.9 = (f32[192,704]{1,0:T(8,128)S(1)}, f32[192,704]{1,0:T(8,128)}, u32[]{:S(2)}) copy-start(f32[192,704]{1,0:T(8,128)} %get-tuple-element.35) | copy-start | bytes 1622020
  131.1 160.1 %reduce-scatter.8.cloned.1.call-start = ((), (), s32[]{:S(2)}) async-start(), calls=%async_computation.4 | async-start | bytes 983040 | tf_op jit(solution)/shard_map/reduce_scatter | solution.py:123
  187.5 77.7 %copy-start.13 = (f32[192,1]{0,1:T(1,128)S(1)}, f32[192,1]{0,1:T(1,128)}, u32[]{:S(2)}) copy-start(f32[192,1]{0,1:T(1,128)} %copy-done.12) | copy-start | bytes 2308
  260.8 4.4 %copy-start.19 = (bf16[1,512,512]{2,1,0:T(8,128)(2,1)S(1)}, bf16[1,512,512]{2,1,0:T(8,128)(2,1)}, u32[]{:S(2)}) copy-start(bf16[1,512,512]{2,1,0:T(8,128)(2,1)} %param.20) | copy-start | bytes 1572868
  260.9 4.4 %copy-start.20 = (bf16[192,512]{1,0:T(8,128)(2,1)S(1)}, bf16[192,512]{1,0:T(8,128)(2,1)}, u32[]{:S(2)}) copy-start(bf16[192,512]{1,0:T(8,128)(2,1)} %param.16) | copy-start | bytes 589828
  262.4 28.8 %copy-start.11 = (bf16[192,512]{1,0:T(8,128)(2,1)S(1)}, bf16[192,512]{1,0:T(8,128)(2,1)}, u32[]{:S(2)}) copy-start(bf16[192,512]{1,0:T(8,128)(2,1)} %param.17) | copy-start | bytes 589828
  (9 other events, 20.8 us)
Sparse Core Ops, SparseCore 0:
  9.5 46.7 all-gather.1
  123.9 59.5 reduce-scatter.11
  187.6 73.2 reduce-scatter.9
  268.8 22.3 reduce-scatter.7
where the time goes:
time: 300 us; the launch traced here: 299 us
  waiting for transfers between devices  180 us (60%)
  matrix products  38.8 us (13%)
  blocking collectives  35 us (12%)
  other arithmetic  16 us (5%)
  local copies, waits for them, and re-layouts  15.6 us (5%)
  between operations  13.7 us (5%)
    reduce_scatter x1, waiting for transfers between devices, query_plan(): lax.psum_scatter((jnp.concatenate(sums, axis=1), jnp.stack(totals, axis=2...  73.3 us
    unnamed x5, waiting for transfers between devices  51.1 us
    pmax x1, blocking collectives, query_plan(): row_max = lax.pmax(jnp.stack(maxima, axis=2), 'tok')  35 us
    all_gather x1, waiting for transfers between devices, query_plan(): all_queries = lax.all_gather(queries, 'tok', axis=0, tiled=True)  33.2 us
    reduce_scatter x1, waiting for transfers between devices, shards(): lax.psum_scatter(projected.astype(jnp.bfloat16), 'grp', scatter_dimension...  22.5 us
    dot_general x4, matrix products, query_plan(): jnp.dot(exps.reshape(dev_count * row_count, -1).astype(jnp.bfloat16), fla...  15 us
    unnamed x65, local copies, waits for them, and re-layouts  9.09 us
    dot_general x4, matrix products, query_plan(): lax.dot_general(all_queries[:, cols], flat_keys[:, cols], (((1,), (1,)),...  8.22 us
  transfers between devices with their start and end apart: 4, of which 4 were waited for; matrix products, arithmetic and copies ran while one was open for 10% of the time, Pallas kernels for 0%

commit v1 on v0

--- a/solution.py
+++ b/solution.py
@@ -194,7 +194,10 @@
     head_width = col_count // head_count
     node_count = upper_keys.shape[0]
     scale = head_width ** (-0.5)
-    all_queries = lax.all_gather(queries, "tok", axis=0, tiled=True)
+    edit_body = lambda local: jnp.concatenate(
+        jax.lax.all_to_all(jnp.stack(jax.lax.axis_size("tok") * [local], axis=0), "tok", 0, 0), 0
+    )
+    all_queries = edit_body(queries)
     req_mid = leaf_mid.astype(jnp.int32)
     req_root = jnp.take(mid_root, req_mid).astype(jnp.int32)
     node_ids = jnp.arange(node_count, dtype=jnp.int32)

time: 300 us -> 299 us (level)
  waiting for transfers between devices: 180 us -> 171 us
  starting transfers between devices: 0.12 us -> 7.37 us
  matrix products: 38.8 us -> 42.3 us
    all_gather x1 -> x0, waiting for transfers between devices: 33.2 us -> none  [query_plan(): all_queries = lax.all_gather(queries, 'tok', axis=0, tiled=True)]
    all_to_all x0 -> x1, waiting for transfers between devices: none -> 24.4 us  [query_plan(): jax.lax.all_to_all(jnp.stack(jax.lax.axis_size('tok') * [local], axis=0),...]
    all_to_all x0 -> x1, starting transfers between devices: none -> 7.25 us  [query_plan(): jax.lax.all_to_all(jnp.stack(jax.lax.axis_size('tok') * [local], axis=0),...]
    dot_general x4, matrix products: 8.22 us -> 11.6 us  [query_plan(): lax.dot_general(all_queries[:, cols], flat_keys[:, cols], (((1,), (1,)),...]
    unnamed x65 -> x73, local copies, waits for them, and re-layouts: 9.09 us -> 7.19 us
    unnamed x5 -> x4, waiting for transfers between devices: 51.1 us -> 50.5 us
  transfers between devices with their start and end apart: 4 -> 4, of which waited for: 4 -> 4; matrix products, arithmetic and copies ran while one was open for 10% -> 9% of each run, Pallas kernels for 0% -> 0%
where the time goes in v1:
time: 299 us
  waiting for transfers between devices  171 us (57%)
  matrix products  42.3 us (14%)
  blocking collectives  35.3 us (12%)
  local copies, waits for them, and re-layouts  14.8 us (5%)
  other arithmetic  14.1 us (5%)
  between operations  13.8 us (5%)
  starting transfers between devices  7.37 us (2%)
    reduce_scatter x1, waiting for transfers between devices, query_plan(): lax.psum_scatter((jnp.concatenate(sums, axis=1), jnp.stack(totals, axis=2...  73.5 us
    unnamed x4, waiting for transfers between devices  50.5 us
    pmax x1, blocking collectives, query_plan(): row_max = lax.pmax(jnp.stack(maxima, axis=2), 'tok')  35.3 us
    all_to_all x1, waiting for transfers between devices, query_plan(): jax.lax.all_to_all(jnp.stack(jax.lax.axis_size('tok') * [local], axis=0),...  24.4 us
    reduce_scatter x1, waiting for transfers between devices, shards(): lax.psum_scatter(projected.astype(jnp.bfloat16), 'grp', scatter_dimension...  22.5 us
    dot_general x4, matrix products, query_plan(): jnp.dot(exps.reshape(dev_count * row_count, -1).astype(jnp.bfloat16), fla...  15 us
    dot_general x4, matrix products, query_plan(): lax.dot_general(all_queries[:, cols], flat_keys[:, cols], (((1,), (1,)),...  11.6 us
    dot_general x4, matrix products, query_plan(): lax.dot_general(queries[:, cols], local_keys[:, cols], (((1,), (1,)), (()...  7.98 us
  transfers between devices with their start and end apart: 4, of which 4 were waited for; matrix products, arithmetic and copies ran while one was open for 9% of the time, Pallas kernels for 0%

profile of v1, /device:TPU:0, one launch (start us, length us, event | category | flops | bytes accessed | tf_op | source)
XLA Modules:
  0.0 298.6 jit_solution(11753949757705351355)
XLA Ops:
  6.6 2.4 stack.49
  8.9 7.3 %all-to-all-start = ((bf16[8,192,512]{2,1,0:T(8,128)(2,1)}), bf16[8,192,512]{2,1,0:T(8,128)(2,1)}, u32[]{:S(2)}, u32[]{:S(2)}) async-start(bf16[8,192,512]{2,1,0:T(8,128)(2,1)} %stack.49), calls=%async_computation | async-start | bytes 3145728 | tf_op jit(solution)/shard_map/all_to_all | solution.py:198
  20.9 2.0 fusion.134
  23.0 2.0 fusion.133
  25.0 2.0 fusion.132
  26.9 2.0 fusion.131
  28.9 24.4 %all-to-all-done = bf16[8,192,512]{2,1,0:T(8,128)(2,1)} async-done(((bf16[8,192,512]{2,1,0:T(8,128)(2,1)}), bf16[8,192,512]{2,1,0:T(8,128)(2,1)}, u32[]{:S(2)}, u32[]{:S(2)}) %all-to-all-start) | async-done | bytes 1572896 | tf_op jit(solution)/shard_map/all_to_all | solution.py:198
  53.3 1.9 fusion.40
  55.2 2.1 fusion.42
  57.3 2.1 fusion.44
  59.4 5.6 %fusion = (f32[1536]{0:T(1024)S(1)}, f32[1536]{0:T(1024)S(1)}, f32[1536]{0:T(1024)S(1)}, f32[1536]{0:T(1024)S(1)}, f32[1536,768]{0,1:T(8,128)}) fusion(pred[1536,768]{0,1:T(32,128)(4,1)S(1)} %copy.27, f32[1536,768]{0,1:T(8,128)S(1)} %fusion.40, f32[1536,768]{0,1:T(8,128)S(1)} %fusion.42, f32[1536,768]{0,1:T(8,128)S(1)} %fusion.44, ...), kind=kOutput, calls=%fused_computation.9 | convolution fusion | flops 316139520 | bytes 20668416 | tf_op jit(solution)/shard_map/dot_general | solution.py:217
  65.8 35.3 %pmax.7 = f32[8,192,4]{1,0,2:T(8,128)S(1)} all-reduce(f32[8,192,4]{1,0,2:T(8,128)S(1)} %pad_maximum_fusion.5), channel_id=1, replica_groups=mesh['tok'=8,'grp'=4] {'tok'}, use_global_device_ids=true, to_apply=%region_10.11 | all-reduce | flops 6144 | bytes 49152 | tf_op jit(solution)/shard_map/pmax | solution.py:242
  101.4 4.9 %fusion.16 = f32[1536,128]{0,1:T(8,128)S(1)} fusion(pred[1536,768]{0,1:T(32,128)(4,1)} %copy-done.5, f32[1536,768]{0,1:T(8,128)} %copy-done.4, f32[1536]{0:T(1024)S(1)} %sub.94, bf16[768,512]{1,0:T(8,128)(2,1)} %bitcast.112), kind=kOutput, calls=%fused_computation.25 | convolution fusion | flops 307888128 | bytes 6887424 | tf_op jit(solution)/shard_map/dot_general | solution.py:251
  106.4 2.3 fusion.14
  108.8 5.4 %fusion.18 = f32[1536,128]{0,1:T(8,128)} fusion(pred[1536,768]{0,1:T(32,128)(4,1)S(1)} %copy-done.6, f32[1536,768]{0,1:T(8,128)} %get-tuple-element.31, f32[1536]{0:T(1024)S(1)} %sub.91, bf16[768,512]{1,0:T(8,128)(2,1)S(1)} %bitcast.114), kind=kOutput, calls=%fused_computation.26 | convolution fusion | flops 307888128 | bytes 6889472 | tf_op jit(solution)/shard_map/dot_general | solution.py:251
  114.2 4.7 %fusion.4 = (f32[1536]{0:T(1024)S(1)}, f32[1536]{0:T(1024)S(1)}, f32[1536]{0:T(1024)S(1)}, f32[1536]{0:T(1024)S(1)}) fusion(pred[1536,768]{0,1:T(32,128)(4,1)S(1)} %copy-done.6, f32[1536,768]{0,1:T(8,128)S(1)} %bitcast.81, f32[1536]{0:T(1024)S(1)} %sub.91, f32[1536]{0:T(1024)S(1)} %sub.100, f32[1536,768]{0,1:T(8,128)S(1)} %bitcast.75, f32[1536]{0:T(1024)S(1)} %sub.97, ...), kind=kLoop, calls=%fused_computation.14 | loop fusion | flops 23586816 | bytes 20103168 | tf_op jit(solution)/shard_map/reduce_sum | solution.py:249
  118.9 2.3 fusion.12
  122.6 3.5 %pad_maximum_fusion = f32[1536,512]{0,1:T(8,128)} fusion(f32[1536,128]{0,1:T(8,128)} %fusion.12, f32[1536,128]{0,1:T(8,128)} %fusion.14, f32[1536,128]{0,1:T(8,128)S(1)} %fusion.16, f32[1536,128]{0,1:T(8,128)} %fusion.18), kind=kLoop, calls=%fused_computation.13 | loop fusion | flops 2359296 | bytes 6291456 | tf_op jit(solution)/shard_map/concatenate | solution.py:259
  126.1 3.7 %copy.43 = f32[1536,512]{1,0:T(8,128)} copy(f32[1536,512]{0,1:T(8,128)} %pad_maximum_fusion) | data formatting | bytes 6291456
  130.0 2.0 fusion.32
  132.0 50.5 %reduce-scatter.12.cloned.1.call-done = f32[192,4]{1,0:T(8,128)} async-done(((f32[1536,4]{1,0:T(8,128)}), f32[192,4]{1,0:T(8,128)}) %reduce-scatter.12.cloned.1.call-update) | async-done | bytes 3088
  186.5 73.5 %reduce-scatter.10.cloned.1.call-done = f32[192,512]{1,0:T(8,128)} async-done(((f32[1536,512]{1,0:T(8,128)}), f32[192,512]{1,0:T(8,128)}) %reduce-scatter.10.cloned.1.call-update) | async-done | bytes 393232 | tf_op jit(solution)/shard_map/reduce_scatter | solution.py:257
  265.7 2.2 convolution_convert_fusion
  267.9 22.5 %reduce-scatter.8.cloned.1.call-done = bf16[192,512]{1,0:T(8,128)(2,1)} async-done(((bf16[192,2048]{1,0:T(8,128)(2,1)}), bf16[192,512]{1,0:T(8,128)(2,1)}) %reduce-scatter.8.cloned.1.call-update) | async-done | bytes 196624 | tf_op jit(solution)/shard_map/reduce_scatter | solution.py:123
  (137 shorter events, 18.4 us)
Async XLA Ops:
  6.5 259.1 %copy-start = (bf16[512,2048]{1,0:T(8,128)(2,1)S(1)}, bf16[512,2048]{1,0:T(8,128)(2,1)}, u32[]{:S(2)}) copy-start(bf16[512,2048]{1,0:T(8,128)(2,1)} %param.18) | copy-start | bytes 6291460
  6.5 9.7 %copy-start.21 = (s32[8]{0:T(128)S(1)}, s32[8]{0:T(128)}, u32[]{:S(2)}) copy-start(s32[8]{0:T(128)} %param.24) | copy-start | bytes 100
  6.5 9.7 %copy-start.1 = (s32[4]{0:T(128)S(1)}, s32[4]{0:T(128)}, u32[]{:S(2)}) copy-start(s32[4]{0:T(128)} %param.25) | copy-start | bytes 52
  6.5 10.4 %copy-start.18 = (s32[6]{0:T(128)S(1)}, s32[6]{0:T(128)}, u32[]{:S(2)}) copy-start(s32[6]{0:T(128)} %param.26) | copy-start | bytes 76
  6.5 12.2 %copy-start.19 = (s32[8]{0:T(128)S(1)}, s32[8]{0:T(128)}, u32[]{:S(2)}) copy-start(s32[8]{0:T(128)} %param.23) | copy-start | bytes 100
  6.5 12.2 %copy-start.20 = (s32[8]{0:T(128)S(1)}, s32[8]{0:T(128)}, u32[]{:S(2)}) copy-start(s32[8]{0:T(128)} %param.27) | copy-start | bytes 100
  6.6 14.4 %copy-start.7 = (bf16[192,512]{1,0:T(8,128)(2,1)S(1)}, bf16[192,512]{1,0:T(8,128)(2,1)}, u32[]{:S(2)}) copy-start(bf16[192,512]{1,0:T(8,128)(2,1)} %param.15) | copy-start | bytes 589828
  8.9 44.4 %all-to-all-start = ((bf16[8,192,512]{2,1,0:T(8,128)(2,1)}), bf16[8,192,512]{2,1,0:T(8,128)(2,1)}, u32[]{:S(2)}, u32[]{:S(2)}) async-start(bf16[8,192,512]{2,1,0:T(8,128)(2,1)} %stack.49), calls=%async_computation | async-start | bytes 3145728 | tf_op jit(solution)/shard_map/all_to_all | solution.py:198
  16.2 166.3 %reduce-scatter.12.cloned.1.call-start = ((), (), s32[]{:S(2)}) async-start(), calls=%async_computation.6 | async-start | bytes 884736
  18.8 40.6 %copy-start.5 = (pred[1536,768]{0,1:T(32,128)(4,1)}, pred[1536,768]{0,1:T(32,128)(4,1)S(1)}, u32[]{:S(2)}) copy-start(pred[1536,768]{0,1:T(32,128)(4,1)S(1)} %copy.27) | copy-start | bytes 3538948
  59.4 5.6 %copy-start.4 = (f32[1536,768]{0,1:T(8,128)}, f32[1536,768]{0,1:T(8,128)S(1)}, u32[]{:S(2)}) copy-start(f32[1536,768]{0,1:T(8,128)S(1)} %fusion.44) | copy-start | bytes 14155780
  101.1 5.2 %slice-start.2 = ((s8[4718592]{0:T(1024)(128)(4,1)}), s8[524288]{0:T(1024)(128)(4,1)S(1)}, s32[]{:S(2)}) async-start(s8[4718592]{0:T(1024)(128)(4,1)} %bitcast.76), calls=%async_computation.9 | async-start | bytes 1048576
  101.4 5.0 %copy-start.6 = (pred[1536,768]{0,1:T(32,128)(4,1)S(1)}, pred[1536,768]{0,1:T(32,128)(4,1)}, u32[]{:S(2)}) copy-start(pred[1536,768]{0,1:T(32,128)(4,1)} %copy-done.5) | copy-start | bytes 3538948
  101.4 5.0 %copy-start.22 = (bf16[6,128,512]{2,1,0:T(8,128)(2,1)S(1)}, bf16[6,128,512]{2,1,0:T(8,128)(2,1)}, u32[]{:S(2)}) copy-start(bf16[6,128,512]{2,1,0:T(8,128)(2,1)} %param.22) | copy-start | bytes 2359300
  106.4 7.8 %slice-start = ((s8[4718592]{0:T(1024)(128)(4,1)}), s8[4194304]{0:T(1024)(128)(4,1)S(1)}, s32[]{:S(2)}) async-start(s8[4718592]{0:T(1024)(128)(4,1)} %bitcast.74), calls=%async_computation.7 | async-start | bytes 8388608
  106.4 7.8 %slice-start.4 = ((s8[4718592]{0:T(1024)(128)(4,1)}), s8[4194304]{0:T(1024)(128)(4,1)S(1)}, s32[]{:S(2)}) async-start(s8[4718592]{0:T(1024)(128)(4,1)} %bitcast.78), calls=%async_computation.11 | async-start | bytes 8388608
  106.4 7.8 %slice-start.6 = ((s8[4718592]{0:T(1024)(128)(4,1)}), s8[4194304]{0:T(1024)(128)(4,1)S(1)}, s32[]{:S(2)}) async-start(s8[4718592]{0:T(1024)(128)(4,1)} %bitcast.80), calls=%async_computation.13 | async-start | bytes 8388608
  108.7 5.4 %slice-start.1 = ((s8[4718592]{0:T(1024)(128)(4,1)}), s8[524288]{0:T(1024)(128)(4,1)S(1)}, s32[]{:S(2)}) async-start(s8[4718592]{0:T(1024)(128)(4,1)} %bitcast.74), calls=%async_computation.8 | async-start | bytes 1048576
  108.7 5.5 %slice-start.5 = ((s8[4718592]{0:T(1024)(128)(4,1)}), s8[524288]{0:T(1024)(128)(4,1)S(1)}, s32[]{:S(2)}) async-start(s8[4718592]{0:T(1024)(128)(4,1)} %bitcast.78), calls=%async_computation.12 | async-start | bytes 1048576
  108.7 5.5 %slice-start.7 = ((s8[4718592]{0:T(1024)(128)(4,1)}), s8[524288]{0:T(1024)(128)(4,1)S(1)}, s32[]{:S(2)}) async-start(s8[4718592]{0:T(1024)(128)(4,1)} %bitcast.80), calls=%async_computation.14 | async-start | bytes 1048576
  122.5 137.5 %reduce-scatter.10.cloned.1.call-start = ((), (), s32[]{:S(2)}) async-start(), calls=%async_computation.5 | async-start | bytes 3538944 | tf_op jit(solution)/shard_map/reduce_scatter | solution.py:257
  129.8 160.6 %reduce-scatter.8.cloned.1.call-start = ((), (), s32[]{:S(2)}) async-start(), calls=%async_computation.4 | async-start | bytes 983040 | tf_op jit(solution)/shard_map/reduce_scatter | solution.py:123
  186.4 78.0 %copy-start.13 = (f32[192,1]{0,1:T(1,128)S(1)}, f32[192,1]{0,1:T(1,128)}, u32[]{:S(2)}) copy-start(f32[192,1]{0,1:T(1,128)} %copy-done.12) | copy-start | bytes 2308
  261.5 28.8 %copy-start.11 = (bf16[192,512]{1,0:T(8,128)(2,1)S(1)}, bf16[192,512]{1,0:T(8,128)(2,1)}, u32[]{:S(2)}) copy-start(bf16[192,512]{1,0:T(8,128)(2,1)} %param.17) | copy-start | bytes 589828
  (13 other events, 41.8 us)
Sparse Core Ops, SparseCore 0:
  122.7 59.7 reduce-scatter.11
  186.5 73.4 reduce-scatter.9
  268.0 22.3 reduce-scatter.7
